TPU v7x, 32 devices: a whole 2x2x4 slice. The times are simulated.
32 devices in a mesh: shot: 4 (over y, core), mesh: 8 (over z, x).
Axes of the slice: x: 2, y: 2, z: 4, core: 2. Of those that a mesh axis runs over, the one named last changes fastest.
Arguments:
- adjoint_state: float32 [4, 13, 35, 1024], P('shot', None, None, 'mesh'), may hold values from -6 to 6
- forward_states: float32 [4, 2, 13, 35, 1024], P('shot', None, None, None, 'mesh'), may hold values from -6 to 6
- material: float32 [6, 35, 1024], P(None, None, 'mesh'), may hold values from 0.5 to 2
- coupling: float32 [3, 6, 13, 13], replicated, may hold values from -0.375 to 0.375
- metric: float32 [3, 3, 1024], P(None, None, 'mesh'), may hold values from -4 to 4
- face_normals: float32 [3, 4, 1024], P(None, None, 'mesh'), may hold values from -4 to 4
- face_scale: float32 [4, 1024], P(None, 'mesh'), may hold values from 1 to 3
- face_neighbours: int32 [4, 1024], P(None, 'mesh'), may hold values from 0 to 639, as said below
- face_orientation: int32 [4, 1024], P(None, 'mesh'), may hold values from 0 to 5
- send_faces: int32 [1024], P('mesh'), may hold values from 0 to 511, as said below
- history_steps: float32 [5, 6, 35, 1024], P(None, None, None, 'mesh')
- history_changes: float32 [5, 6, 35, 1024], P(None, None, None, 'mesh'), as said below
Outputs:
- adjoint_final: float32 [4, 13, 35, 1024], P('shot', None, None, 'mesh')
- direction: float32 [6, 35, 1024], P(None, None, ('mesh', 'shot'))
Inputs may be any that keep to these rules, and one draw needn't show every extreme that they name: `face_neighbours`: local faces of a partition are numbered x * 128 + e. Each face either forms a pair with another local face (each names the other) or reads exactly one of the 128 ghost slots, and every ghost slot is read by exactly one face; on every partition the face that reads slot 512 + j is send_faces[j] and the face that reads slot 576 + j is send_faces[64 + j]. `send_faces`: the 128 entries of one partition are distinct local face numbers. `history_changes`: for every stored pair, s_i . y_i is positive.
All inputs are finite; a program needn't handle non-finite values.
Results may differ from a plain program's by a relative error of at most 0.0003.
Values sent between devices are 32-bit elements; how exact they have to be, the bound alone decides.
No kernel may reach another device: no remote copies, remote signals or barrier semaphores. Data moves between devices by JAX's collectives and lax.ppermute only.
A program may use at most 64 MiB of HBM per device.

v0:
```python
import math
import jax
import jax.numpy as jnp
import numpy as np
from jax import lax
from jax.sharding import PartitionSpec as P

HIGH = lax.Precision.HIGHEST
STEP_SIZE = 0.02


def padded(x, sides, width):
    for axis, dim in sides:
        devices, length = (lax.axis_size(axis), x.shape[dim])
        up = [(i, (i + 1) % devices) for i in range(devices - 1)]
        down = [(j, i) for i, j in up]
        last = lax.slice_in_dim(x, length - width, length, axis=dim)
        first = lax.slice_in_dim(x, 0, width, axis=dim)
        before = lax.ppermute(last, axis, up)
        after = lax.ppermute(first, axis, down)
        x = jnp.concatenate([before, x, after], axis=dim)
    return x


def invert_matrix(matrix):
    order_count = matrix.shape[0]
    working = np.concatenate([matrix * 1.0, np.eye(order_count)], axis=1)
    for column in range(order_count):
        pivot_row = column + int(np.argmax(np.abs(working[column:, column])))
        working[[column, pivot_row]] = working[[pivot_row, column]]
        working[column] = working[column] / working[column, column]
        for target in range(order_count):
            if target != column:
                working[target] = working[target] - working[target, column] * working[column]
    return working[:, order_count:]


def basis_tables():
    points = [
        (across, along, upward)
        for upward in range(5)
        for along in range(5 - upward)
        for across in range(5 - upward - along)
    ]
    exponents = np.array(points) * 1.0
    coords = exponents / 4.0
    vander = np.prod(coords[:, None, :] ** exponents[None, :, :], axis=2)
    inverse = invert_matrix(vander)
    derivs = []
    for direction_axis in range(3):
        lowered = np.maximum(exponents - np.eye(3)[direction_axis], 0.0)
        slopes = exponents[None, :, direction_axis] * np.prod(
            coords[:, None, :] ** lowered[None, :, :], axis=2
        )
        derivs.append(slopes @ inverse)
    moments = np.array(
        [
            [
                math.factorial(first[0] + second[0])
                * math.factorial(first[1] + second[1])
                * math.factorial(first[2] + second[2])
                / math.factorial(sum(first) + sum(second) + 3)
                for second in points
            ]
            for first in points
        ]
    )
    mass_matrix = inverse.T @ moments @ inverse
    lattice = [(across, along) for along in range(5) for across in range(5 - along)]
    lattice_powers = np.array(lattice) * 1.0
    face_vander = np.prod((lattice_powers / 4.0)[:, None, :] ** lattice_powers[None, :, :], axis=2)
    face_inverse = invert_matrix(face_vander)
    face_moments = np.array(
        [
            [
                math.factorial(first[0] + second[0])
                * math.factorial(first[1] + second[1])
                / math.factorial(sum(first) + sum(second) + 2)
                for second in lattice
            ]
            for first in lattice
        ]
    )
    face_mass = face_inverse.T @ face_moments @ face_inverse
    numbers = {point: number for number, point in enumerate(points)}
    face_points = [
        [(across, along, 0) for across, along in lattice],
        [(across, 0, along) for across, along in lattice],
        [(0, across, along) for across, along in lattice],
        [(across, along, 4 - across - along) for across, along in lattice],
    ]
    face_nodes = np.array(
        [[numbers[point] for point in listing] for listing in face_points], np.int32
    )
    mass_inverse = invert_matrix(mass_matrix)
    lift_tables = []
    for face_number in range(4):
        selector = np.eye(35)[face_nodes[face_number]]
        lift_tables.append(mass_inverse @ selector.T @ face_mass)
    orderings = [(0, 1, 2), (1, 2, 0), (2, 0, 1), (1, 0, 2), (0, 2, 1), (2, 1, 0)]
    lattice_numbers = {point: number for number, point in enumerate(lattice)}
    triples = [(across, along, 4 - across - along) for across, along in lattice]
    turn_nodes = np.array(
        [
            [lattice_numbers[triple[ordering[0]], triple[ordering[1]]] for triple in triples]
            for ordering in orderings
        ],
        np.int32,
    )
    return (
        jnp.asarray(np.stack(derivs), jnp.float32),
        jnp.asarray(np.stack(lift_tables), jnp.float32),
        face_nodes,
        turn_nodes,
    )


def spatial_of(field, metric, derivs):
    reference_grads = jnp.einsum("rab,fbe->rfae", derivs, field, precision=HIGH)
    rows = []
    for direction_axis in range(3):
        total = metric[0, direction_axis] * reference_grads[0]
        total = total + metric[1, direction_axis] * reference_grads[1]
        total = total + metric[2, direction_axis] * reference_grads[2]
        rows.append(total)
    return jnp.stack(rows)


def volume_term(adjoint, material, coupling, metric, derivs):
    spatial = spatial_of(adjoint, metric, derivs)
    mixing = jnp.einsum("dpfg,dfae->pgae", coupling, spatial, precision=HIGH)
    return jnp.sum(material[:, None] * mixing, axis=0)


def kernel_term(adjoint, forward, coupling, metric, derivs):
    spatial = spatial_of(forward, metric, derivs)
    mixing = jnp.einsum("dpfg,dgae->pfae", coupling, spatial, precision=HIGH)
    return jnp.sum(mixing * adjoint[None], axis=1)


def surface_term(jump_trace, face_material, face_normals, face_scale, coupling, lift_tables):
    weighted = face_normals[:, None, None] * jump_trace[None]
    mixing = jnp.einsum("dpfg,dfnxe->pgnxe", coupling, weighted, precision=HIGH)
    face_flux = 0.5 * jnp.sum(face_material[:, None] * mixing, axis=0) + 0.5 * jump_trace
    return jnp.einsum(
        "xan,fnxe->fae", lift_tables, face_flux * face_scale[None, None], precision=HIGH
    )


def search_direction(total_grad, step_rows, change_rows, combine_sums):
    pairs = step_rows.shape[0]
    summed = combine_sums(
        jnp.concatenate(
            [
                jnp.sum(step_rows * change_rows, axis=(1, 2, 3)),
                jnp.sum(change_rows[pairs - 1] * change_rows[pairs - 1])[None],
            ]
        )
    )
    curvature = summed[:pairs]
    alphas = [None] * pairs
    work = total_grad
    for slot in reversed(range(pairs)):
        alphas[slot] = combine_sums(jnp.sum(step_rows[slot] * work)) / curvature[slot]
        work = work - alphas[slot] * change_rows[slot]
    work = curvature[pairs - 1] / summed[pairs] * work
    for slot in range(pairs):
        beta_now = combine_sums(jnp.sum(change_rows[slot] * work)) / curvature[slot]
        work = work + (alphas[slot] - beta_now) * step_rows[slot]
    return -work


def shards(
    adjoint_state,
    forward_states,
    material,
    coupling,
    metric,
    face_normals,
    face_scale,
    face_neighbours,
    face_orientation,
    send_faces,
    history_steps,
    history_changes,
):
    derivs, lift_tables, face_nodes, turn_nodes = basis_tables()
    fields = adjoint_state.shape[1]
    elements = adjoint_state.shape[3]
    node_count = material.shape[1]
    params = material.shape[0]
    face_width = face_nodes.shape[1]
    border = send_faces.shape[0] // 2
    slot_count = 4 * elements + 2 * border
    adjoint = adjoint_state[0]
    face_material = material[:, face_nodes.T, :]
    neighbours = face_neighbours.reshape(-1)
    orient = face_orientation.reshape(-1)
    node_pick = jnp.zeros((face_width, 4 * elements), jnp.int32)
    for option in range(turn_nodes.shape[0]):
        node_pick = (
            node_pick
            + (orient == option).astype(jnp.int32)[None, :]
            * jnp.asarray(turn_nodes[option], jnp.int32)[:, None]
        )
    flat_index = (node_pick * slot_count + neighbours[None, :]).reshape(-1)
    gradient = jnp.zeros((params, node_count, elements), jnp.float32)
    for step_index in range(forward_states.shape[1]):
        inner_trace = adjoint[:, face_nodes.T, :]
        flat_trace = inner_trace.reshape(fields, face_width, 4 * elements)
        sent_traces = flat_trace[:, :, send_faces]
        extended = padded(sent_traces, (("mesh", 2),), border)
        ghosts = jnp.concatenate(
            [flat_trace, extended[:, :, :border], extended[:, :, 3 * border :]], axis=2
        )
        turned = ghosts.reshape(fields, face_width * slot_count)[:, flat_index]
        jump_trace = turned.reshape(fields, face_width, 4, elements) - inner_trace
        change = volume_term(adjoint, material, coupling, metric, derivs) + surface_term(
            jump_trace, face_material, face_normals, face_scale, coupling, lift_tables
        )
        adjoint = adjoint + STEP_SIZE * change
        gradient = gradient + STEP_SIZE * kernel_term(
            adjoint, forward_states[0, step_index], coupling, metric, derivs
        )
    total_grad = lax.psum(gradient, "shot")

    def combine_sums(values):
        return lax.psum(values, "mesh")

    result = search_direction(total_grad, history_steps, history_changes, combine_sums)
    share_width = elements // lax.axis_size("shot")
    result = lax.dynamic_slice_in_dim(result, lax.axis_index("shot") * share_width, share_width, 2)
    return (adjoint[None], result)


def solution(mesh):
    placed = (
        P("shot", None, None, "mesh"),
        P("shot", None, None, None, "mesh"),
        P(None, None, "mesh"),
        P(),
        P(None, None, "mesh"),
        P(None, None, "mesh"),
        P(None, "mesh"),
        P(None, "mesh"),
        P(None, "mesh"),
        P("mesh"),
        P(None, None, None, "mesh"),
        P(None, None, None, "mesh"),
    )
    return jax.shard_map(
        shards,
        mesh=mesh,
        in_specs=placed,
        out_specs=(P("shot", None, None, "mesh"), P(None, None, ("mesh", "shot"))),
        check_vma=False,
    )
```

profile of v0, /device:TPU:0, one launch (start us, length us, event | category | flops | bytes accessed | tf_op | source)
XLA Modules:
  0.0 404.9 jit_solution(5043594300675908869)
XLA Ops:
  9.8 3.6 copy.157
  13.5 3.8 gather_fusion.2
  17.4 2.4 fusion.84
  21.2 6.3 %collective-permute-start = (f32[13,15,64]{1,0,2:T(8,128)}, f32[13,15,64]{1,0,2:T(8,128)}, u32[]{:S(2)}, u32[]{:S(2)}) collective-permute-start(f32[13,15,64]{1,0,2:T(8,128)} %get-tuple-element.22), channel_id=1, source_target_pairs={{0,1},{1,2},{2,3},{3,4},{4,5},{5,6},{6,7},{8,9},{9,10},{10,11},{11... | collective-permute-start | bytes 149768 | tf_op jit(solution)/shard_map/ppermute | solution.py:19
  33.5 2.3 fusion.5
  40.8 7.6 %collective-permute-done = f32[13,15,64]{1,0,2:T(8,128)} collective-permute-done((f32[13,15,64]{1,0,2:T(8,128)}, f32[13,15,64]{1,0,2:T(8,128)}, u32[]{:S(2)}, u32[]{:S(2)}) %collective-permute-start) | collective-permute-done | bytes 49952 | tf_op jit(solution)/shard_map/ppermute | solution.py:19
  49.8 3.2 copy.160
  53.0 17.3 %gather_fusion.3 = f32[7680,13]{1,0:T(8,128)} fusion(f32[13,9600]{0,1:T(8,128)} %bitcast.349, s32[8192]{0:T(1024)S(1)} %pad_clamp_fusion), kind=kCustom, calls=%fused_computation.3 | custom fusion | bytes 829440 | tf_op jit(solution)/shard_map/gather | solution.py:216
  70.3 2.7 copy.161
  73.1 3.6 fusion.1
  81.2 3.6 copy.170
  84.8 3.9 gather_fusion.5
  92.2 5.8 %collective-permute-start.2 = (f32[13,15,64]{1,0,2:T(8,128)}, f32[13,15,64]{1,0,2:T(8,128)}, u32[]{:S(2)}, u32[]{:S(2)}) collective-permute-start(f32[13,15,64]{1,0,2:T(8,128)} %get-tuple-element.20), channel_id=1, source_target_pairs={{0,1},{1,2},{2,3},{3,4},{4,5},{5,6},{6,7},{8,9},{9,10},{10,11},{11... | collective-permute-start | bytes 149768 | tf_op jit(solution)/shard_map/ppermute | solution.py:19
  98.2 2.4 fusion.3
  100.7 2.3 fusion.4
  103.0 4.5 %collective-permute-done.3 = f32[13,15,64]{1,0,2:T(8,128)} collective-permute-done((f32[13,15,64]{1,0,2:T(8,128)S(1)}, f32[13,15,64]{1,0,2:T(8,128)}, u32[]{:S(2)}, u32[]{:S(2)}) %collective-permute-start.3) | collective-permute-done | bytes 49952 | tf_op jit(solution)/shard_map/ppermute | solution.py:20
  108.7 10.1 %collective-permute-done.2 = f32[13,15,64]{1,0,2:T(8,128)} collective-permute-done((f32[13,15,64]{1,0,2:T(8,128)}, f32[13,15,64]{1,0,2:T(8,128)}, u32[]{:S(2)}, u32[]{:S(2)}) %collective-permute-start.2) | collective-permute-done | bytes 49952 | tf_op jit(solution)/shard_map/ppermute | solution.py:19
  120.2 3.2 copy.173
  123.5 17.3 %gather_fusion.6 = f32[7680,13]{1,0:T(8,128)} fusion(f32[13,9600]{0,1:T(8,128)} %bitcast.348, s32[8192]{0:T(1024)S(1)} %pad_clamp_fusion), kind=kCustom, calls=%fused_computation.6 | custom fusion | bytes 829440 | tf_op jit(solution)/shard_map/gather | solution.py:216
  140.8 2.8 copy.174
  143.7 2.7 fusion
  150.6 31.2 %all-reduce.3.cloned.1.call-done = f32[6,35,128]{2,0,1:T(8,128)} async-done(((f32[6,35,128]{2,0,1:T(8,128)}), f32[6,35,128]{2,0,1:T(8,128)}) %all-reduce.3.cloned.1.call-update) | async-done | bytes 107536 | tf_op jit(solution)/shard_map/psum | solution.py:225
  183.3 22.0 %all-reduce = (f32[]{:T(128)}, f32[6]{0:T(128)S(1)}) all-reduce(f32[]{:T(128)} %multiply_reduce_fusion.1, f32[6]{0:T(128)S(1)} %pad_maximum_fusion.2), channel_id=1, replica_groups=mesh['shot'=4,'mesh'=8] {'mesh'}, use_global_device_ids=true, to_apply=%region_11.0 | all-reduce | flops 7 | bytes 56 | tf_op jit(solution)/shard_map/psum | solution.py:228
  208.8 17.8 %psum.87 = f32[]{:T(128)} all-reduce(f32[]{:T(128)} %fusion.63), channel_id=1, replica_groups=mesh['shot'=4,'mesh'=8] {'mesh'}, use_global_device_ids=true, to_apply=%region_13.0 | all-reduce | flops 1 | bytes 8 | tf_op jit(solution)/shard_map/psum | solution.py:228
  229.5 19.7 %psum.88 = f32[]{:T(128)} all-reduce(f32[]{:T(128)} %get-tuple-element.18), channel_id=1, replica_groups=mesh['shot'=4,'mesh'=8] {'mesh'}, use_global_device_ids=true, to_apply=%region_15.0 | all-reduce | flops 1 | bytes 8 | tf_op jit(solution)/shard_map/psum | solution.py:228
  251.2 17.8 %psum.89 = f32[]{:T(128)} all-reduce(f32[]{:T(128)} %fusion.47), channel_id=1, replica_groups=mesh['shot'=4,'mesh'=8] {'mesh'}, use_global_device_ids=true, to_apply=%region_17.0 | all-reduce | flops 1 | bytes 8 | tf_op jit(solution)/shard_map/psum | solution.py:228
  271.0 19.7 %psum.90 = f32[]{:T(128)} all-reduce(f32[]{:T(128)} %get-tuple-element.16), channel_id=1, replica_groups=mesh['shot'=4,'mesh'=8] {'mesh'}, use_global_device_ids=true, to_apply=%region_19.0 | all-reduce | flops 1 | bytes 8 | tf_op jit(solution)/shard_map/psum | solution.py:228
  294.1 17.8 %psum.91 = f32[]{:T(128)} all-reduce(f32[]{:T(128)} %fusion.36), channel_id=1, replica_groups=mesh['shot'=4,'mesh'=8] {'mesh'}, use_global_device_ids=true, to_apply=%region_21.0 | all-reduce | flops 1 | bytes 8 | tf_op jit(solution)/shard_map/psum | solution.py:228
  313.9 19.8 %psum.92 = f32[]{:T(128)} all-reduce(f32[]{:T(128)} %fusion.44), channel_id=1, replica_groups=mesh['shot'=4,'mesh'=8] {'mesh'}, use_global_device_ids=true, to_apply=%region_23.0 | all-reduce | flops 1 | bytes 8 | tf_op jit(solution)/shard_map/psum | solution.py:228
  335.7 17.7 %psum.93 = f32[]{:T(128)} all-reduce(f32[]{:T(128)} %get-tuple-element.14), channel_id=1, replica_groups=mesh['shot'=4,'mesh'=8] {'mesh'}, use_global_device_ids=true, to_apply=%region_25.0 | all-reduce | flops 1 | bytes 8 | tf_op jit(solution)/shard_map/psum | solution.py:228
  356.3 19.7 %psum.94 = f32[]{:T(128)} all-reduce(f32[]{:T(128)} %fusion.60), channel_id=1, replica_groups=mesh['shot'=4,'mesh'=8] {'mesh'}, use_global_device_ids=true, to_apply=%region_27.0 | all-reduce | flops 1 | bytes 8 | tf_op jit(solution)/shard_map/psum | solution.py:228
  378.1 17.7 %psum.95 = f32[]{:T(128)} all-reduce(f32[]{:T(128)} %get-tuple-element.12), channel_id=1, replica_groups=mesh['shot'=4,'mesh'=8] {'mesh'}, use_global_device_ids=true, to_apply=%region_29.0 | all-reduce | flops 1 | bytes 8 | tf_op jit(solution)/shard_map/psum | solution.py:228
  (147 shorter events, 43.0 us)
Async XLA Ops:
  7.2 174.6 %all-reduce.3.cloned.1.call-start = ((), (), s32[]{:S(2)}) async-start(), calls=%async_computation | async-start | bytes 286720 | tf_op jit(solution)/shard_map/psum | solution.py:225
  9.5 4.0 copy-start.35
  9.8 17.7 %copy-start.2 = (f32[5,6,35,128]{3,2,1,0:T(8,128)S(1)}, f32[5,6,35,128]{3,2,1,0:T(8,128)}, u32[]{:S(2)}) copy-start(f32[5,6,35,128]{3,2,1,0:T(8,128)} %param.37) | copy-start | bytes 1612804
  9.8 17.7 %copy-start.3 = (f32[5,6,35,128]{3,2,1,0:T(8,128)S(1)}, f32[5,6,35,128]{3,2,1,0:T(8,128)}, u32[]{:S(2)}) copy-start(f32[5,6,35,128]{3,2,1,0:T(8,128)} %param.36) | copy-start | bytes 1612804
  13.5 3.9 copy-start.23
  13.5 15.6 %copy-start.26 = (s32[4,128]{1,0:T(4,128)S(1)}, s32[4,128]{1,0:T(4,128)}, u32[]{:S(2)}) copy-start(s32[4,128]{1,0:T(4,128)} %param.34) | copy-start | bytes 6148
  17.3 11.8 %copy-start.27 = (s32[4,128]{1,0:T(4,128)S(1)}, s32[4,128]{1,0:T(4,128)}, u32[]{:S(2)}) copy-start(s32[4,128]{1,0:T(4,128)} %param.33) | copy-start | bytes 6148
  17.3 11.8 %copy-start.30 = (s32[15]{0:T(128)S(1)}, s32[15]{0:T(128)}, u32[]{:S(2)}) copy-start(s32[15]{0:T(128)} %constant.67.clone) | copy-start | bytes 184
  17.3 11.8 %copy-start.31 = (s32[15]{0:T(128)S(1)}, s32[15]{0:T(128)}, u32[]{:S(2)}) copy-start(s32[15]{0:T(128)} %constant.66.clone) | copy-start | bytes 184
  17.3 11.8 %copy-start.32 = (s32[15]{0:T(128)S(1)}, s32[15]{0:T(128)}, u32[]{:S(2)}) copy-start(s32[15]{0:T(128)} %constant.65.clone) | copy-start | bytes 184
  17.3 11.8 %copy-start.33 = (s32[15]{0:T(128)S(1)}, s32[15]{0:T(128)}, u32[]{:S(2)}) copy-start(s32[15]{0:T(128)} %constant.64.clone) | copy-start | bytes 184
  17.3 11.8 %copy-start.34 = (s32[15]{0:T(128)S(1)}, s32[15]{0:T(128)}, u32[]{:S(2)}) copy-start(s32[15]{0:T(128)} %constant.63.clone) | copy-start | bytes 184
  17.4 12.0 %copy-start.28 = (f32[4,128]{1,0:T(4,128)S(1)}, f32[4,128]{1,0:T(4,128)}, u32[]{:S(2)}) copy-start(f32[4,128]{1,0:T(4,128)} %param.32) | copy-start | bytes 6148
  17.4 12.0 %copy-start.1 = (f32[1,13,35,128]{3,0,2,1:T(1,128)S(1)}, f32[1,13,35,128]{3,0,2,1:T(1,128)}, u32[]{:S(2)}) copy-start(f32[1,13,35,128]{3,0,2,1:T(1,128)} %param.26) | copy-start | bytes 698884
  17.4 12.0 %copy-start.10 = (f32[3,35,35,1]{2,1,3,0:T(8,128)S(1)}, f32[3,35,35,1]{2,1,3,0:T(8,128)}, u32[]{:S(2)}) copy-start(f32[3,35,35,1]{2,1,3,0:T(8,128)} %constant.74) | copy-start | bytes 44104
  19.8 10.5 %copy-start.25 = (f32[3,3,128]{2,1,0:T(4,128)S(1)}, f32[3,3,128]{2,1,0:T(4,128)}, u32[]{:S(2)}) copy-start(f32[3,3,128]{2,1,0:T(4,128)} %param.30) | copy-start | bytes 13828
  19.8 10.5 %copy-start = (f32[6,35,128]{2,1,0:T(8,128)S(1)}, f32[6,35,128]{2,1,0:T(8,128)}, u32[]{:S(2)}) copy-start(f32[6,35,128]{2,1,0:T(8,128)} %param.28) | copy-start | bytes 322564
  19.8 10.5 %copy-start.16 = (f32[1,2,13,35,128]{4,1,3,2,0:T(2,128)S(1)}, f32[1,2,13,35,128]{4,1,3,2,0:T(2,128)}, u32[]{:S(2)}) copy-start(f32[1,2,13,35,128]{4,1,3,2,0:T(2,128)} %param.27) | copy-start | bytes 1397764
  19.8 19.8 %collective-permute-start.1 = (f32[13,15,64]{1,0,2:T(8,128)}, f32[13,15,64]{1,0,2:T(8,128)}, u32[]{:S(2)}, u32[]{:S(2)}) collective-permute-start(f32[13,15,64]{1,0,2:T(8,128)} %get-tuple-element.23), channel_id=1, source_target_pairs={{1,0},{2,1},{3,2},{4,3},{5,4},{6,5},{7,6},{9,8},{10,9},{11,10},{12... | collective-permute-start | bytes 149768 | tf_op jit(solution)/shard_map/ppermute | solution.py:20
  21.2 27.2 %collective-permute-start = (f32[13,15,64]{1,0,2:T(8,128)}, f32[13,15,64]{1,0,2:T(8,128)}, u32[]{:S(2)}, u32[]{:S(2)}) collective-permute-start(f32[13,15,64]{1,0,2:T(8,128)} %get-tuple-element.22), channel_id=1, source_target_pairs={{0,1},{1,2},{2,3},{3,4},{4,5},{5,6},{6,7},{8,9},{9,10},{10,11},{11... | collective-permute-start | bytes 149768 | tf_op jit(solution)/shard_map/ppermute | solution.py:19
  35.8 3.7 copy-start.24
  39.6 33.6 %copy-start.21 = (f32[3,4,128]{2,0,1:T(4,128)}, f32[3,4,128]{2,0,1:T(4,128)S(1)}, u32[]{:S(2)}) copy-start(f32[3,4,128]{2,0,1:T(4,128)S(1)} %copy.154) | copy-start | bytes 18436
  73.0 3.8 copy-start.8
  73.0 3.8 copy-start.19
  88.7 9.4 %copy-start.12 = (f32[3,13,35,128,1]{3,2,1,0,4:T(8,128)S(1)}, f32[3,13,35,128,1]{3,2,1,0,4:T(8,128)}, u32[]{:S(2)}) copy-start(f32[3,13,35,128,1]{3,2,1,0,4:T(8,128)} %maximum_bitcast_fusion.2) | copy-start | bytes 2096644
  88.7 9.4 %copy-start.14 = (f32[3,6,13,13]{3,2,1,0:T(8,128)S(1)}, f32[3,6,13,13]{3,2,1,0:T(8,128)}, u32[]{:S(2)}) copy-start(f32[3,6,13,13]{3,2,1,0:T(8,128)} %param.29) | copy-start | bytes 36508
  90.9 16.6 %collective-permute-start.3 = (f32[13,15,64]{1,0,2:T(8,128)S(1)}, f32[13,15,64]{1,0,2:T(8,128)}, u32[]{:S(2)}, u32[]{:S(2)}) collective-permute-start(f32[13,15,64]{1,0,2:T(8,128)S(1)} %get-tuple-element.21), channel_id=1, source_target_pairs={{1,0},{2,1},{3,2},{4,3},{5,4},{6,5},{7,6},{9,8},{10,9},{11,10},{12... | collective-permute-start | bytes 149768 | tf_op jit(solution)/shard_map/ppermute | solution.py:20
  92.2 26.7 %collective-permute-start.2 = (f32[13,15,64]{1,0,2:T(8,128)}, f32[13,15,64]{1,0,2:T(8,128)}, u32[]{:S(2)}, u32[]{:S(2)}) collective-permute-start(f32[13,15,64]{1,0,2:T(8,128)} %get-tuple-element.20), channel_id=1, source_target_pairs={{0,1},{1,2},{2,3},{3,4},{4,5},{5,6},{6,7},{8,9},{9,10},{10,11},{11... | collective-permute-start | bytes 149768 | tf_op jit(solution)/shard_map/ppermute | solution.py:19
  146.4 4.1 %copy-start.6 = (f32[1,6,35,128]{3,2,1,0:T(8,128)S(1)}, f32[1,6,35,128]{3,2,1,0:T(8,128)}, u32[]{:S(2)}) copy-start(f32[1,6,35,128]{3,2,1,0:T(8,128)} %get-tuple-element.69) | copy-start | bytes 322564
  146.5 81.4 %copy-start.4 = (f32[1,6,35,128]{3,2,1,0:T(8,128)S(1)}, f32[1,6,35,128]{3,2,1,0:T(8,128)}, u32[]{:S(2)}) copy-start(f32[1,6,35,128]{3,2,1,0:T(8,128)} %get-tuple-element.39) | copy-start | bytes 322564
  146.6 104.0 %copy-start.5 = (f32[1,6,35,128]{3,2,1,0:T(8,128)S(1)}, f32[1,6,35,128]{3,2,1,0:T(8,128)}, u32[]{:S(2)}) copy-start(f32[1,6,35,128]{3,2,1,0:T(8,128)} %get-tuple-element.72) | copy-start | bytes 322564
  146.6 123.8 %copy-start.7 = (f32[1,6,35,128]{3,2,1,0:T(8,128)S(1)}, f32[1,6,35,128]{3,2,1,0:T(8,128)}, u32[]{:S(2)}) copy-start(f32[1,6,35,128]{3,2,1,0:T(8,128)} %get-tuple-element.37) | copy-start | bytes 322564
  (9 other events, 26.3 us)
Sparse Core Ops, SparseCore 0:
  150.0 31.6 all-reduce.2
where the time goes:
time: 406 us; the launch traced here: 405 us
  blocking collectives  190 us (47%)
  local copies, waits for them, and re-layouts  81.3 us (20%)
  waiting for transfers between devices  53.4 us (13%)
  between operations  29.4 us (7%)
  matrix products  19.9 us (5%)
  other arithmetic  16.3 us (4%)
  starting transfers between devices  14.9 us (4%)
    psum x10, blocking collectives, combine_sums(): return lax.psum(values, 'mesh')  190 us
    gather x2, local copies, waits for them, and re-layouts, shards(): turned = ghosts.reshape(fields, face_width * slot_count)[:, flat_index]  34.6 us
    psum x1, waiting for transfers between devices, shards(): total_grad = lax.psum(gradient, 'shot')  31.2 us
    ppermute x2, waiting for transfers between devices, padded(): before = lax.ppermute(last, axis, up)  17.7 us
    ppermute x2, starting transfers between devices, padded(): before = lax.ppermute(last, axis, up)  12.1 us
    reshape x4, local copies, waits for them, and re-layouts, shards(): flat_trace = inner_trace.reshape(fields, face_width, 4 * elements)  8.56 us
  transfers between devices with their start and end apart: 5, of which 4 were waited for; matrix products, arithmetic and copies ran while one was open for 5% of the time, Pallas kernels for 0%

commit v1 on v0

--- a/solution.py
+++ b/solution.py
@@ -222,7 +222,11 @@
         gradient = gradient + STEP_SIZE * kernel_term(
             adjoint, forward_states[0, step_index], coupling, metric, derivs
         )
-    total_grad = lax.psum(gradient, "shot")
+    total_grad = gradient
+    for hop in (1, 2):
+        total_grad = total_grad + lax.ppermute(
+            total_grad, "shot", [(dev, dev ^ hop) for dev in range(4)]
+        )
 
     def combine_sums(values):
         return lax.psum(values, "mesh")

time: 406 us -> 363 us (0.89)
  waiting for transfers between devices: 53.4 us -> 26.4 us
  between operations: 29.4 us -> 15.9 us
    psum x1 -> x0, waiting for transfers between devices: 31.2 us -> none  [shards(): total_grad = lax.psum(gradient, 'shot')]
    ppermute x0 -> x2, waiting for transfers between devices: none -> 4.28 us  [shards(): lax.ppermute(total_grad, 'shot', [(dev, dev ^ hop) for dev in range(4)])]
  transfers between devices with their start and end apart: 5 -> 6, of which waited for: 4 -> 5; matrix products, arithmetic and copies ran while one was open for 5% -> 6% of each run, Pallas kernels for 0% -> 0%
where the time goes in v1:
time: 363 us; the launch traced here: 362 us
  blocking collectives  189 us (52%)
  local copies, waits for them, and re-layouts  82 us (23%)
  waiting for transfers between devices  26.4 us (7%)
  matrix products  19.9 us (5%)
  starting transfers between devices  16.5 us (5%)
  between operations  15.9 us (4%)
  other arithmetic  13.1 us (4%)
    psum x10, blocking collectives, combine_sums(): return lax.psum(values, 'mesh')  189 us
    gather x2, local copies, waits for them, and re-layouts, shards(): turned = ghosts.reshape(fields, face_width * slot_count)[:, flat_index]  34.6 us
    ppermute x2, waiting for transfers between devices, padded(): before = lax.ppermute(last, axis, up)  17.6 us
    ppermute x2, starting transfers between devices, padded(): before = lax.ppermute(last, axis, up)  12.2 us
    reshape x4, local copies, waits for them, and re-layouts, shards(): flat_trace = inner_trace.reshape(fields, face_width, 4 * elements)  8.56 us
    gather x2, local copies, waits for them, and re-layouts, shards(): sent_traces = flat_trace[:, :, send_faces]  7.74 us
  transfers between devices with their start and end apart: 6, of which 5 were waited for; matrix products, arithmetic and copies ran while one was open for 6% of the time, Pallas kernels for 0%

profile of v1, /device:TPU:0, one launch (start us, length us, event | category | flops | bytes accessed | tf_op | source)
XLA Modules:
  0.0 362.4 jit_solution(15135836400248404411)
XLA Ops:
  3.3 3.6 copy.157
  6.9 3.8 %gather_fusion.2 = f32[128,13,15]{2,1,0:T(8,128)} fusion(f32[13,15,512]{1,0,2:T(8,128)} %copy.157, s32[1024]{0:T(1024)S(1)} %pad_clamp_fusion.1), kind=kCustom, calls=%fused_computation.2 | custom fusion | bytes 200192 | tf_op jit(solution)/shard_map/gather | solution.py:211
  10.8 2.4 fusion.84
  14.6 6.3 %collective-permute-start = (f32[13,15,64]{1,0,2:T(8,128)}, f32[13,15,64]{1,0,2:T(8,128)}, u32[]{:S(2)}, u32[]{:S(2)}) collective-permute-start(f32[13,15,64]{1,0,2:T(8,128)} %get-tuple-element.24), channel_id=1, source_target_pairs={{0,1},{1,2},{2,3},{3,4},{4,5},{5,6},{6,7},{8,9},{9,10},{10,11},{11... | collective-permute-start | bytes 149768 | tf_op jit(solution)/shard_map/ppermute | solution.py:19
  26.3 2.3 fusion.5
  34.3 7.5 %collective-permute-done = f32[13,15,64]{1,0,2:T(8,128)} collective-permute-done((f32[13,15,64]{1,0,2:T(8,128)}, f32[13,15,64]{1,0,2:T(8,128)}, u32[]{:S(2)}, u32[]{:S(2)}) %collective-permute-start) | collective-permute-done | bytes 49952 | tf_op jit(solution)/shard_map/ppermute | solution.py:19
  43.2 3.2 copy.160
  46.4 17.3 %gather_fusion.3 = f32[7680,13]{1,0:T(8,128)} fusion(f32[13,9600]{0,1:T(8,128)} %bitcast.349, s32[8192]{0:T(1024)S(1)} %pad_clamp_fusion), kind=kCustom, calls=%fused_computation.3 | custom fusion | bytes 829440 | tf_op jit(solution)/shard_map/gather | solution.py:216
  63.7 2.7 copy.161
  66.6 3.6 %fusion.1 = f32[13,15,4,128]{3,0,2,1:T(8,128)S(1)} fusion(f32[6,15,4,128]{3,0,2,1:T(8,128)} %bitcast.361, f32[13,15,4,128]{3,0,2,1:T(8,128)S(1)} %sub.44, f32[3,4,128]{2,0,1:T(4,128)S(1)} %copy.154, f32[3,6,13,13]{3,2,1,0:T(8,128)S(1)} %copy-done.13), kind=kOutput, calls=%fused_computation.10 | convolution fusion | flops 281748480 | bytes 1001352 | tf_op jit(solution)/shard_map/dpfg,dfnxe->pgnxe/dot_general | solution.py:143
  74.6 3.6 copy.170
  78.2 3.9 %gather_fusion.5 = f32[128,13,15]{2,1,0:T(8,128)} fusion(f32[13,15,512]{1,0,2:T(8,128)} %copy.170, s32[1024]{0:T(1024)} %copy-done.24), kind=kCustom, calls=%fused_computation.5 | custom fusion | bytes 200192 | tf_op jit(solution)/shard_map/gather | solution.py:211
  85.6 5.8 %collective-permute-start.2 = (f32[13,15,64]{1,0,2:T(8,128)}, f32[13,15,64]{1,0,2:T(8,128)}, u32[]{:S(2)}, u32[]{:S(2)}) collective-permute-start(f32[13,15,64]{1,0,2:T(8,128)} %get-tuple-element.22), channel_id=1, source_target_pairs={{0,1},{1,2},{2,3},{3,4},{4,5},{5,6},{6,7},{8,9},{9,10},{10,11},{11... | collective-permute-start | bytes 149768 | tf_op jit(solution)/shard_map/ppermute | solution.py:19
  91.6 2.4 fusion.3
  94.1 2.3 fusion.4
  96.4 4.5 %collective-permute-done.3 = f32[13,15,64]{1,0,2:T(8,128)} collective-permute-done((f32[13,15,64]{1,0,2:T(8,128)S(1)}, f32[13,15,64]{1,0,2:T(8,128)}, u32[]{:S(2)}, u32[]{:S(2)}) %collective-permute-start.3) | collective-permute-done | bytes 49952 | tf_op jit(solution)/shard_map/ppermute | solution.py:20
  102.2 10.1 %collective-permute-done.2 = f32[13,15,64]{1,0,2:T(8,128)} collective-permute-done((f32[13,15,64]{1,0,2:T(8,128)}, f32[13,15,64]{1,0,2:T(8,128)}, u32[]{:S(2)}, u32[]{:S(2)}) %collective-permute-start.2) | collective-permute-done | bytes 49952 | tf_op jit(solution)/shard_map/ppermute | solution.py:19
  113.7 3.2 copy.173
  116.9 17.3 %gather_fusion.6 = f32[7680,13]{1,0:T(8,128)} fusion(f32[13,9600]{0,1:T(8,128)} %bitcast.348, s32[8192]{0:T(1024)S(1)} %pad_clamp_fusion), kind=kCustom, calls=%fused_computation.6 | custom fusion | bytes 829440 | tf_op jit(solution)/shard_map/gather | solution.py:216
  134.2 2.8 copy.174
  137.1 2.7 fusion
  146.4 3.6 collective-permute-done.5
  150.6 20.9 %all-reduce = (f32[]{:T(128)}, f32[6]{0:T(128)S(1)}) all-reduce(f32[]{:T(128)} %get-tuple-element.20, f32[6]{0:T(128)S(1)} %pad_maximum_fusion.2), channel_id=1, replica_groups=mesh['shot'=4,'mesh'=8] {'mesh'}, use_global_device_ids=true, to_apply=%region_10.0 | all-reduce | flops 7 | bytes 56 | tf_op jit(solution)/shard_map/psum | solution.py:232
  174.2 17.8 %psum.79 = f32[]{:T(128)} all-reduce(f32[]{:T(128)} %fusion.63), channel_id=1, replica_groups=mesh['shot'=4,'mesh'=8] {'mesh'}, use_global_device_ids=true, to_apply=%region_12.0 | all-reduce | flops 1 | bytes 8 | tf_op jit(solution)/shard_map/psum | solution.py:232
  193.9 19.7 %psum.80 = f32[]{:T(128)} all-reduce(f32[]{:T(128)} %get-tuple-element.18), channel_id=1, replica_groups=mesh['shot'=4,'mesh'=8] {'mesh'}, use_global_device_ids=true, to_apply=%region_14.0 | all-reduce | flops 1 | bytes 8 | tf_op jit(solution)/shard_map/psum | solution.py:232
  215.7 17.8 %psum.81 = f32[]{:T(128)} all-reduce(f32[]{:T(128)} %fusion.47), channel_id=1, replica_groups=mesh['shot'=4,'mesh'=8] {'mesh'}, use_global_device_ids=true, to_apply=%region_16.0 | all-reduce | flops 1 | bytes 8 | tf_op jit(solution)/shard_map/psum | solution.py:232
  235.4 19.7 %psum.82 = f32[]{:T(128)} all-reduce(f32[]{:T(128)} %get-tuple-element.16), channel_id=1, replica_groups=mesh['shot'=4,'mesh'=8] {'mesh'}, use_global_device_ids=true, to_apply=%region_18.0 | all-reduce | flops 1 | bytes 8 | tf_op jit(solution)/shard_map/psum | solution.py:232
  258.4 17.8 %psum.83 = f32[]{:T(128)} all-reduce(f32[]{:T(128)} %fusion.36), channel_id=1, replica_groups=mesh['shot'=4,'mesh'=8] {'mesh'}, use_global_device_ids=true, to_apply=%region_20.0 | all-reduce | flops 1 | bytes 8 | tf_op jit(solution)/shard_map/psum | solution.py:232
  278.2 19.7 %psum.84 = f32[]{:T(128)} all-reduce(f32[]{:T(128)} %fusion.44), channel_id=1, replica_groups=mesh['shot'=4,'mesh'=8] {'mesh'}, use_global_device_ids=true, to_apply=%region_22.0 | all-reduce | flops 1 | bytes 8 | tf_op jit(solution)/shard_map/psum | solution.py:232
  299.9 17.8 %psum.85 = f32[]{:T(128)} all-reduce(f32[]{:T(128)} %get-tuple-element.14), channel_id=1, replica_groups=mesh['shot'=4,'mesh'=8] {'mesh'}, use_global_device_ids=true, to_apply=%region_24.0 | all-reduce | flops 1 | bytes 8 | tf_op jit(solution)/shard_map/psum | solution.py:232
  320.6 19.7 %psum.86 = f32[]{:T(128)} all-reduce(f32[]{:T(128)} %fusion.60), channel_id=1, replica_groups=mesh['shot'=4,'mesh'=8] {'mesh'}, use_global_device_ids=true, to_apply=%region_26.0 | all-reduce | flops 1 | bytes 8 | tf_op jit(solution)/shard_map/psum | solution.py:232
  342.3 17.8 %psum.87 = f32[]{:T(128)} all-reduce(f32[]{:T(128)} %get-tuple-element.12), channel_id=1, replica_groups=mesh['shot'=4,'mesh'=8] {'mesh'}, use_global_device_ids=true, to_apply=%region_28.0 | all-reduce | flops 1 | bytes 8 | tf_op jit(solution)/shard_map/psum | solution.py:232
  (151 shorter events, 42.7 us)
Async XLA Ops:
  2.9 4.0 %copy-start.36 = (s32[128]{0:T(128)S(1)}, s32[128]{0:T(128)}, u32[]{:S(2)}) copy-start(s32[128]{0:T(128)} %param.35) | copy-start | bytes 1540
  3.2 17.7 %copy-start.2 = (f32[5,6,35,128]{3,2,1,0:T(8,128)S(1)}, f32[5,6,35,128]{3,2,1,0:T(8,128)}, u32[]{:S(2)}) copy-start(f32[5,6,35,128]{3,2,1,0:T(8,128)} %param.37) | copy-start | bytes 1612804
  3.3 17.7 %copy-start.3 = (f32[5,6,35,128]{3,2,1,0:T(8,128)S(1)}, f32[5,6,35,128]{3,2,1,0:T(8,128)}, u32[]{:S(2)}) copy-start(f32[5,6,35,128]{3,2,1,0:T(8,128)} %param.36) | copy-start | bytes 1612804
  6.9 3.9 %copy-start.24 = (s32[1024]{0:T(1024)}, s32[1024]{0:T(1024)S(1)}, u32[]{:S(2)}) copy-start(s32[1024]{0:T(1024)S(1)} %pad_clamp_fusion.1) | copy-start | bytes 12292
  6.9 15.6 %copy-start.27 = (s32[4,128]{1,0:T(4,128)S(1)}, s32[4,128]{1,0:T(4,128)}, u32[]{:S(2)}) copy-start(s32[4,128]{1,0:T(4,128)} %param.34) | copy-start | bytes 6148
  10.7 11.8 %copy-start.28 = (s32[4,128]{1,0:T(4,128)S(1)}, s32[4,128]{1,0:T(4,128)}, u32[]{:S(2)}) copy-start(s32[4,128]{1,0:T(4,128)} %param.33) | copy-start | bytes 6148
  10.7 11.8 %copy-start.31 = (s32[15]{0:T(128)S(1)}, s32[15]{0:T(128)}, u32[]{:S(2)}) copy-start(s32[15]{0:T(128)} %constant.67.clone) | copy-start | bytes 184
  10.7 11.8 %copy-start.32 = (s32[15]{0:T(128)S(1)}, s32[15]{0:T(128)}, u32[]{:S(2)}) copy-start(s32[15]{0:T(128)} %constant.66.clone) | copy-start | bytes 184
  10.7 11.8 %copy-start.33 = (s32[15]{0:T(128)S(1)}, s32[15]{0:T(128)}, u32[]{:S(2)}) copy-start(s32[15]{0:T(128)} %constant.65.clone) | copy-start | bytes 184
  10.8 11.8 %copy-start.34 = (s32[15]{0:T(128)S(1)}, s32[15]{0:T(128)}, u32[]{:S(2)}) copy-start(s32[15]{0:T(128)} %constant.64.clone) | copy-start | bytes 184
  10.8 11.8 %copy-start.35 = (s32[15]{0:T(128)S(1)}, s32[15]{0:T(128)}, u32[]{:S(2)}) copy-start(s32[15]{0:T(128)} %constant.63.clone) | copy-start | bytes 184
  10.8 12.0 %copy-start.29 = (f32[4,128]{1,0:T(4,128)S(1)}, f32[4,128]{1,0:T(4,128)}, u32[]{:S(2)}) copy-start(f32[4,128]{1,0:T(4,128)} %param.32) | copy-start | bytes 6148
  10.8 12.0 %copy-start.1 = (f32[1,13,35,128]{3,0,2,1:T(1,128)S(1)}, f32[1,13,35,128]{3,0,2,1:T(1,128)}, u32[]{:S(2)}) copy-start(f32[1,13,35,128]{3,0,2,1:T(1,128)} %param.26) | copy-start | bytes 698884
  10.8 12.0 %copy-start.10 = (f32[3,35,35,1]{2,1,3,0:T(8,128)S(1)}, f32[3,35,35,1]{2,1,3,0:T(8,128)}, u32[]{:S(2)}) copy-start(f32[3,35,35,1]{2,1,3,0:T(8,128)} %constant.74) | copy-start | bytes 44104
  13.2 10.5 %copy-start.26 = (f32[3,3,128]{2,1,0:T(4,128)S(1)}, f32[3,3,128]{2,1,0:T(4,128)}, u32[]{:S(2)}) copy-start(f32[3,3,128]{2,1,0:T(4,128)} %param.30) | copy-start | bytes 13828
  13.2 10.5 %copy-start = (f32[6,35,128]{2,1,0:T(8,128)S(1)}, f32[6,35,128]{2,1,0:T(8,128)}, u32[]{:S(2)}) copy-start(f32[6,35,128]{2,1,0:T(8,128)} %param.28) | copy-start | bytes 322564
  13.2 10.6 %copy-start.17 = (f32[1,2,13,35,128]{4,1,3,2,0:T(2,128)S(1)}, f32[1,2,13,35,128]{4,1,3,2,0:T(2,128)}, u32[]{:S(2)}) copy-start(f32[1,2,13,35,128]{4,1,3,2,0:T(2,128)} %param.27) | copy-start | bytes 1397764
  13.2 19.8 %collective-permute-start.1 = (f32[13,15,64]{1,0,2:T(8,128)}, f32[13,15,64]{1,0,2:T(8,128)}, u32[]{:S(2)}, u32[]{:S(2)}) collective-permute-start(f32[13,15,64]{1,0,2:T(8,128)} %get-tuple-element.25), channel_id=1, source_target_pairs={{1,0},{2,1},{3,2},{4,3},{5,4},{6,5},{7,6},{9,8},{10,9},{11,10},{12... | collective-permute-start | bytes 149768 | tf_op jit(solution)/shard_map/ppermute | solution.py:20
  14.6 27.2 %collective-permute-start = (f32[13,15,64]{1,0,2:T(8,128)}, f32[13,15,64]{1,0,2:T(8,128)}, u32[]{:S(2)}, u32[]{:S(2)}) collective-permute-start(f32[13,15,64]{1,0,2:T(8,128)} %get-tuple-element.24), channel_id=1, source_target_pairs={{0,1},{1,2},{2,3},{3,4},{4,5},{5,6},{6,7},{8,9},{9,10},{10,11},{11... | collective-permute-start | bytes 149768 | tf_op jit(solution)/shard_map/ppermute | solution.py:19
  32.4 34.2 %copy-start.22 = (f32[3,4,128]{2,0,1:T(4,128)}, f32[3,4,128]{2,0,1:T(4,128)S(1)}, u32[]{:S(2)}) copy-start(f32[3,4,128]{2,0,1:T(4,128)S(1)} %copy.154) | copy-start | bytes 18436
  82.2 9.4 %copy-start.12 = (f32[3,13,35,128,1]{3,2,1,0,4:T(8,128)S(1)}, f32[3,13,35,128,1]{3,2,1,0,4:T(8,128)}, u32[]{:S(2)}) copy-start(f32[3,13,35,128,1]{3,2,1,0,4:T(8,128)} %maximum_bitcast_fusion.2) | copy-start | bytes 2096644
  82.2 9.4 %copy-start.14 = (f32[3,6,13,13]{3,2,1,0:T(8,128)S(1)}, f32[3,6,13,13]{3,2,1,0:T(8,128)}, u32[]{:S(2)}) copy-start(f32[3,6,13,13]{3,2,1,0:T(8,128)} %param.29) | copy-start | bytes 36508
  84.3 16.6 %collective-permute-start.3 = (f32[13,15,64]{1,0,2:T(8,128)S(1)}, f32[13,15,64]{1,0,2:T(8,128)}, u32[]{:S(2)}, u32[]{:S(2)}) collective-permute-start(f32[13,15,64]{1,0,2:T(8,128)S(1)} %get-tuple-element.23), channel_id=1, source_target_pairs={{1,0},{2,1},{3,2},{4,3},{5,4},{6,5},{7,6},{9,8},{10,9},{11,10},{12... | collective-permute-start | bytes 149768 | tf_op jit(solution)/shard_map/ppermute | solution.py:20
  85.6 26.7 %collective-permute-start.2 = (f32[13,15,64]{1,0,2:T(8,128)}, f32[13,15,64]{1,0,2:T(8,128)}, u32[]{:S(2)}, u32[]{:S(2)}) collective-permute-start(f32[13,15,64]{1,0,2:T(8,128)} %get-tuple-element.22), channel_id=1, source_target_pairs={{0,1},{1,2},{2,3},{3,4},{4,5},{5,6},{6,7},{8,9},{9,10},{10,11},{11... | collective-permute-start | bytes 149768 | tf_op jit(solution)/shard_map/ppermute | solution.py:19
  139.8 5.8 %copy-start.30 = (f32[5]{0:T(128)S(1)}, f32[5]{0:T(128)}, u32[]{:S(2)}) copy-start(f32[5]{0:T(128)} %multiply_reduce_fusion) | copy-start | bytes 64
  140.0 33.5 %copy-start.4 = (f32[1,6,35,128]{3,2,1,0:T(8,128)S(1)}, f32[1,6,35,128]{3,2,1,0:T(8,128)}, u32[]{:S(2)}) copy-start(f32[1,6,35,128]{3,2,1,0:T(8,128)} %get-tuple-element.72) | copy-start | bytes 322564
  140.0 53.3 %copy-start.5 = (f32[1,6,35,128]{3,2,1,0:T(8,128)S(1)}, f32[1,6,35,128]{3,2,1,0:T(8,128)}, u32[]{:S(2)}) copy-start(f32[1,6,35,128]{3,2,1,0:T(8,128)} %get-tuple-element.41) | copy-start | bytes 322564
  140.0 75.0 %copy-start.6 = (f32[1,6,35,128]{3,2,1,0:T(8,128)S(1)}, f32[1,6,35,128]{3,2,1,0:T(8,128)}, u32[]{:S(2)}) copy-start(f32[1,6,35,128]{3,2,1,0:T(8,128)} %get-tuple-element.74) | copy-start | bytes 322564
  140.7 93.9 %copy-start.7 = (f32[1,6,35,128]{3,2,1,0:T(8,128)S(1)}, f32[1,6,35,128]{3,2,1,0:T(8,128)}, u32[]{:S(2)}) copy-start(f32[1,6,35,128]{3,2,1,0:T(8,128)} %get-tuple-element.39) | copy-start | bytes 322564
  142.6 1.4 collective-permute-start.4
  144.1 217.3 %copy-start.16 = (f32[1,6,35,128]{3,1,2,0:T(8,128)S(1)}, f32[1,6,35,128]{3,1,2,0:T(8,128)}, u32[]{:S(2)}) copy-start(f32[1,6,35,128]{3,1,2,0:T(8,128)} %copy.411) | copy-start | bytes 322564
  144.1 5.9 %collective-permute-start.5 = (f32[6,35,128]{2,0,1:T(8,128)S(1)}, f32[6,35,128]{2,0,1:T(8,128)S(1)}, u32[]{:S(2)}, u32[]{:S(2)}) collective-permute-start(f32[6,35,128]{2,0,1:T(8,128)S(1)} %add.309), channel_id=1, source_target_pairs={{0,16},{8,24},{16,0},{24,8},{1,17},{9,25},{17,1},{25,9},{2,18},{10... | collective-permute-start | bytes 322568 | tf_op jit(solution)/shard_map/ppermute | solution.py:227
  (11 other events, 33.6 us)
